TPU v7x, 512 devices: a whole 4x8x8 slice. The times are simulated.
512 devices in a mesh: seq: 16 (over y, x_lo), chan: 32 (over z, x_hi, core).
Axes of the slice: x: 4 (x_hi: 2, x_lo: 2; x = x_hi * 2 + x_lo), y: 8, z: 8, core: 2. Of those that a mesh axis runs over, the one named last changes fastest.
Arguments:
- stream_in: bfloat16 [2048, 8192], P('seq', 'chan'), may hold values from -64 to 64
- outer_gate: bfloat16 [2048, 8192], P('seq', 'chan'), may hold values from -4 to 4
- inner_gate: bfloat16 [2048, 8192], P('seq', 'chan'), may hold values from -4 to 4
- values: bfloat16 [2048, 8192], P('seq', 'chan'), may hold values from -4 to 4
- long_filter: bfloat16 [2048, 8192], P('seq', 'chan'), may hold values from -1.2 to 1.2
- norm_gain: float32 [8192], P('chan'), may hold values from 0.5 to 1.5
- cotangent: bfloat16 [2048, 8192], P('seq', 'chan'), may hold values from -16 to 16
Outputs:
- normed: bfloat16 [2048, 8192], P('seq', 'chan')
- stream_grad: bfloat16 [2048, 8192], P('seq', 'chan')
- outer_grad: bfloat16 [2048, 8192], P('seq', 'chan')
- inner_grad: bfloat16 [2048, 8192], P('seq', 'chan')
- value_grad: bfloat16 [2048, 8192], P('seq', 'chan')
All inputs are finite; a program needn't handle non-finite values.
Results may differ from a plain program's by a relative error of at most 0.012.
Values may be sent and summed in bfloat16 or wider, within the bound.
No kernel may reach another device: no remote copies, remote signals or barrier semaphores. Data moves between devices by JAX's collectives and lax.ppermute only.
A program may use at most 64 MiB of HBM per device.

v0:
```python
import math
import jax
import jax.numpy as jnp
from jax import lax
from jax.sharding import PartitionSpec as P

EPSILON = 1e-06
HIGHEST_MODE = lax.Precision.HIGHEST


def from_behind(value, axis, steps):
    count = lax.axis_size(axis)
    first, last = (max(0, -steps), min(count, count - steps))
    return lax.ppermute(value, axis, [(source, source + steps) for source in range(first, last)])


def shortened(shard):

    def short(part):
        return part.astype(jnp.bfloat16) if part.dtype == jnp.float32 else part

    return jax.tree.map(short, shard)


def dft_tables(half):
    length = 2 * half
    rows = lax.broadcasted_iota(jnp.int32, (length, length), 0)
    cols = lax.broadcasted_iota(jnp.int32, (length, length), 1)
    step = math.pi / half
    phase = (rows % half * cols % length).astype(jnp.float32) * step
    nyquist = (half * cols % length).astype(jnp.float32) * step
    forward = jnp.where(
        rows < half, jnp.cos(phase), jnp.where(rows == half, jnp.cos(nyquist), -jnp.sin(phase))
    )
    phase_back = (cols % half * rows % length).astype(jnp.float32) * step
    nyquist_back = (half * rows % length).astype(jnp.float32) * step
    weight = jnp.where(cols == 0, 1.0, 2.0)
    inverse = jnp.where(
        cols < half,
        weight * jnp.cos(phase_back),
        jnp.where(cols == half, jnp.cos(nyquist_back), -2.0 * jnp.sin(phase_back)),
    )
    return (forward, inverse / length)


def spectral_product(left, right, conjugate):
    half = left.shape[-2] // 2
    left_real, left_imag = (left[..., :half, :], left[..., half:, :])
    right_real, right_imag = (right[..., :half, :], right[..., half:, :])
    first_bin = lax.broadcasted_iota(jnp.int32, (half, 1), 0) == 0
    if conjugate:
        right_eff = jnp.where(first_bin, right_imag, -right_imag)
    else:
        right_eff = right_imag
    real_out = left_real * right_real - jnp.where(first_bin, 0.0, left_imag * right_eff)
    imag_out = jnp.where(
        first_bin, left_imag * right_imag, left_real * right_eff + left_imag * right_real
    )
    return jnp.concatenate([real_out, imag_out], axis=-2)


def matmul_high(left, right):
    return jnp.dot(left, right, precision=HIGHEST_MODE, preferred_element_type=jnp.float32)


def body(stream_in, outer_gate, inner_gate, values, long_filter, norm_gain, cotangent):
    half = stream_in.shape[0]
    width = stream_in.shape[1]
    forward, inverse = dft_tables(half)
    forward_half = forward[:, :half]
    outer = outer_gate.astype(jnp.float32)
    inner = inner_gate.astype(jnp.float32)
    value_rows = values.astype(jnp.float32)
    token_position = lax.axis_index("seq")
    devices = lax.axis_size("seq")
    mixed = inner * value_rows
    data_spec = matmul_high(forward_half, mixed).astype(jnp.bfloat16)
    own_spec = matmul_high(forward_half, long_filter.astype(jnp.float32)).astype(jnp.bfloat16)
    filt_spec = lax.all_gather(own_spec[None], "seq", axis=0, tiled=True)
    zero_total = jnp.zeros((2 * half, width), jnp.float32)
    piece = lax.all_gather(data_spec[None], "seq", axis=0, tiled=True)

    def forward_one_block(offset, inner_total):
        lag = token_position - offset
        taps = lax.dynamic_index_in_dim(filt_spec, jnp.clip(lag, 0, devices - 1), 0, keepdims=False)
        block = lax.dynamic_index_in_dim(piece, offset, 0, keepdims=False)
        term = spectral_product(block.astype(jnp.float32), taps.astype(jnp.float32), False)
        return inner_total + jnp.where(lag >= 0, term, 0.0)

    total = lax.fori_loop(0, piece.shape[0], forward_one_block, zero_total)
    waveform = matmul_high(inverse, total)
    spill = from_behind(waveform[half:].astype(jnp.bfloat16), "seq", 1).astype(jnp.float32)
    conv = waveform[:half] + spill
    resid = stream_in.astype(jnp.float32) + outer * conv
    scaled = cotangent.astype(jnp.float32) * norm_gain
    square_sum, proj_sum = lax.psum(
        (
            jnp.sum(resid * resid, axis=1, keepdims=True),
            jnp.sum(scaled * resid, axis=1, keepdims=True),
        ),
        "chan",
    )
    total_width = width * lax.axis_size("chan")
    inv_rms = lax.rsqrt(square_sum / total_width + EPSILON)
    normed = (resid * inv_rms * norm_gain).astype(jnp.bfloat16)
    grad_resid = inv_rms * (scaled - resid * inv_rms * inv_rms * (proj_sum / total_width))
    outer_grad = (grad_resid * conv).astype(jnp.bfloat16)
    dconv = grad_resid * outer
    following = from_behind(shortened(dconv), "seq", -1).astype(dconv.dtype)
    back_spec = matmul_high(forward, jnp.concatenate([dconv, following], axis=0)).astype(
        jnp.bfloat16
    )
    backward_piece = lax.all_gather(back_spec[None], "seq", axis=0, tiled=True)

    def backward_one_block(offset, inner_total):
        lag = offset - token_position
        taps = lax.dynamic_index_in_dim(filt_spec, jnp.clip(lag, 0, devices - 1), 0, keepdims=False)
        block = lax.dynamic_index_in_dim(backward_piece, offset, 0, keepdims=False)
        term = spectral_product(block.astype(jnp.float32), taps.astype(jnp.float32), True)
        return inner_total + jnp.where(lag >= 0, term, 0.0)

    back_total = lax.fori_loop(
        0, backward_piece.shape[0], backward_one_block, jnp.zeros((2 * half, width), jnp.float32)
    )
    dmixed = matmul_high(inverse[:half], back_total)
    inner_grad = (dmixed * value_rows).astype(jnp.bfloat16)
    value_grad = (dmixed * inner).astype(jnp.bfloat16)
    return (normed, grad_resid.astype(jnp.bfloat16), outer_grad, inner_grad, value_grad)


def solution(mesh):
    placed = (
        P("seq", "chan"),
        P("seq", "chan"),
        P("seq", "chan"),
        P("seq", "chan"),
        P("seq", "chan"),
        P("chan"),
        P("seq", "chan"),
    )
    return jax.shard_map(
        body,
        mesh=mesh,
        in_specs=placed,
        out_specs=(
            P("seq", "chan"),
            P("seq", "chan"),
            P("seq", "chan"),
            P("seq", "chan"),
            P("seq", "chan"),
        ),
        check_vma=False,
    )
```

profile of v0, /device:TPU:4, one launch (start us, length us, event | category | flops | bytes accessed | tf_op | source)
XLA Modules:
  0.0 370.6 jit_solution(12434627319497629787)
XLA Ops:
  7.3 2.7 select_multiply_fusion
  10.0 0.9 convolution_convert_fusion.1
  11.0 1.9 convolution_convert_fusion.2
  13.0 77.7 %all-gather.9.cloned.1.call-done = bf16[4096,256]{1,0:T(8,128)(2,1)} async-done(((bf16[256,256]{1,0:T(8,128)(2,1)}), bf16[4096,256]{1,0:T(8,128)(2,1)}) %all-gather.9.cloned.1.call-update) | async-done | bytes 2097168 | tf_op jit(solution)/shard_map/all_gather | solution.py:79
  90.7 76.4 %all-gather.7.cloned.1.call-done = bf16[4096,256]{1,0:T(8,128)(2,1)} async-done(((bf16[256,256]{1,0:T(8,128)(2,1)}), bf16[4096,256]{1,0:T(8,128)(2,1)}) %all-gather.7.cloned.1.call-update) | async-done | bytes 2097168 | tf_op jit(solution)/shard_map/all_gather | solution.py:81
  167.0 19.8 %while.28 = (s32[]{:T(128)}, f32[256,256]{1,0:T(8,128)S(1)}, s32[]{:T(128)}, bf16[16,256,256]{2,1,0:T(8,128)(2,1)}, bf16[16,256,256]{2,1,0:T(8,128)(2,1)}, /*index=5*/s32[]{:T(128)}, s32[]{:T(128)}, s32[]{:T(128)}) while((s32[]{:T(128)}, f32[256,256]{1,0:T(8,128)S(1)}, s32[]{:T(128)}, bf16[16,256,256]{2,1,0:T(8,128)(2,1)}, ...), condition=%wide.region_1.2_spmd.clone, body=%wide.region_0.1_spmd.clone.sunk | while | flops 655495 | bytes 2359701 | solution.py:90
  167.0 1.0 dynamic-slice_convert_fusion.6
  168.3 1.0 dynamic-slice_convert_fusion.6
  169.5 1.0 dynamic-slice_convert_fusion.6
  170.7 1.0 dynamic-slice_convert_fusion.6
  172.0 1.0 dynamic-slice_convert_fusion.6
  173.2 1.0 dynamic-slice_convert_fusion.6
  174.5 1.0 dynamic-slice_convert_fusion.6
  175.7 1.0 dynamic-slice_convert_fusion.6
  176.9 1.0 dynamic-slice_convert_fusion.6
  178.2 1.0 dynamic-slice_convert_fusion.6
  179.4 1.0 dynamic-slice_convert_fusion.6
  180.7 1.0 dynamic-slice_convert_fusion.6
  181.9 1.0 dynamic-slice_convert_fusion.6
  183.1 1.0 dynamic-slice_convert_fusion.6
  184.4 1.0 dynamic-slice_convert_fusion.6
  185.6 1.0 dynamic-slice_convert_fusion.6
  186.9 2.2 fusion.23
  189.1 1.5 collective-permute-start
  191.0 1.5 collective-permute-done
  192.6 60.3 %all-reduce = (f32[128,1]{0,1:T(1,128)S(1)}, f32[128,1]{0,1:T(1,128)S(1)}) all-reduce(f32[128,1]{0,1:T(1,128)S(1)} %bitcast.65, f32[128,1]{0,1:T(1,128)S(1)} %bitcast.64), channel_id=1, replica_groups=mesh['seq'=16,'chan'=32] {'chan'}, use_global_device_ids=true, to_apply=%region_3.4 | all-reduce | flops 256 | bytes 2048 | tf_op jit(solution)/shard_map/psum | solution.py:96
  253.1 1.3 collective-permute-start.1
  254.4 5.6 %collective-permute-done.1 = bf16[128,256]{0,1:T(8,128)(2,1)S(1)} collective-permute-done((bf16[128,256]{0,1:T(8,128)(2,1)S(1)}, bf16[128,256]{0,1:T(8,128)(2,1)S(1)}, u32[]{:S(2)}, u32[]{:S(2)}) %collective-permute-start.1) | collective-permute-done | bytes 65568 | tf_op jit(solution)/shard_map/ppermute | solution.py:14
  260.0 2.2 convolution_convert_fusion
  264.5 78.4 %all-gather.11.cloned.1.call-done = bf16[4096,256]{1,0:T(8,128)(2,1)} async-done(((bf16[256,256]{1,0:T(8,128)(2,1)}), bf16[4096,256]{1,0:T(8,128)(2,1)}) %all-gather.11.cloned.1.call-update) | async-done | bytes 2097168 | tf_op jit(solution)/shard_map/all_gather | solution.py:113
  343.0 20.1 %while.29 = (s32[]{:T(128)}, f32[256,256]{1,0:T(8,128)S(1)}, s32[]{:T(128)}, bf16[16,256,256]{2,1,0:T(8,128)(2,1)}, bf16[16,256,256]{2,1,0:T(8,128)(2,1)}, /*index=5*/s32[]{:T(128)}, s32[]{:T(128)}, s32[]{:T(128)}) while((s32[]{:T(128)}, f32[256,256]{1,0:T(8,128)S(1)}, s32[]{:T(128)}, bf16[16,256,256]{2,1,0:T(8,128)(2,1)}, ...), condition=%wide.region_7.8_spmd.clone, body=%wide.region_6.7_spmd.clone.sunk | while | flops 753799 | bytes 2359701 | solution.py:122
  343.0 1.0 dynamic-slice_convert_fusion.7
  344.3 1.0 dynamic-slice_convert_fusion.7
  345.5 1.0 dynamic-slice_convert_fusion.7
  346.8 1.0 dynamic-slice_convert_fusion.7
  348.0 1.0 dynamic-slice_convert_fusion.7
  349.3 1.0 dynamic-slice_convert_fusion.7
  350.5 1.0 dynamic-slice_convert_fusion.7
  351.8 1.0 dynamic-slice_convert_fusion.7
  353.0 1.0 dynamic-slice_convert_fusion.7
  354.3 1.0 dynamic-slice_convert_fusion.7
  355.6 1.0 dynamic-slice_convert_fusion.7
  356.8 1.0 dynamic-slice_convert_fusion.7
  358.1 1.0 dynamic-slice_convert_fusion.7
  359.3 1.0 dynamic-slice_convert_fusion.7
  360.6 1.0 dynamic-slice_convert_fusion.7
  361.8 1.0 dynamic-slice_convert_fusion.7
  363.1 0.9 fusion.13
  (135 shorter events, 9.0 us)
Async XLA Ops:
  7.2 2.8 copy-start
  7.2 83.5 %all-gather.9.cloned.1.call-start = ((), (), s32[]{:S(2)}) async-start(), calls=%async_computation.1 | async-start | bytes 2228224 | tf_op jit(solution)/shard_map/all_gather | solution.py:79
  10.9 156.1 %all-gather.7.cloned.1.call-start = ((), (), s32[]{:S(2)}) async-start(), calls=%async_computation | async-start | bytes 2228224 | tf_op jit(solution)/shard_map/all_gather | solution.py:81
  12.9 330.1 %all-gather.11.cloned.1.call-start = ((), (), s32[]{:S(2)}) async-start(), calls=%async_computation.2 | async-start | bytes 2228224 | tf_op jit(solution)/shard_map/all_gather | solution.py:113
  186.8 3.8 %copy-start.3 = (bf16[128,256]{1,0:T(8,128)(2,1)S(1)}, bf16[128,256]{1,0:T(8,128)(2,1)}, u32[]{:S(2)}) copy-start(bf16[128,256]{1,0:T(8,128)(2,1)} %param.12) | copy-start | bytes 196612
  186.8 3.9 %copy-start.4 = (bf16[128,256]{1,0:T(8,128)(2,1)S(1)}, bf16[128,256]{1,0:T(8,128)(2,1)}, u32[]{:S(2)}) copy-start(bf16[128,256]{1,0:T(8,128)(2,1)} %param.17) | copy-start | bytes 196612
  186.9 4.0 %copy-start.5 = (bf16[128,256]{1,0:T(8,128)(2,1)S(1)}, bf16[128,256]{1,0:T(8,128)(2,1)}, u32[]{:S(2)}) copy-start(bf16[128,256]{1,0:T(8,128)(2,1)} %param.11) | copy-start | bytes 196612
  186.9 5.6 %copy-start.6 = (f32[256]{0:T(256)S(1)}, f32[256]{0:T(256)}, u32[]{:S(2)}) copy-start(f32[256]{0:T(256)} %param.16) | copy-start | bytes 3076
  189.1 3.4 collective-permute-start
  253.1 6.9 %collective-permute-start.1 = (bf16[128,256]{0,1:T(8,128)(2,1)S(1)}, bf16[128,256]{0,1:T(8,128)(2,1)S(1)}, u32[]{:S(2)}, u32[]{:S(2)}) collective-permute-start(bf16[128,256]{0,1:T(8,128)(2,1)S(1)} %get-tuple-element.260), channel_id=1, source_target_pairs={{32,0},{64,32},{96,64},{128,96},{160,128},{192,160},{224,192},{256... | collective-permute-start | bytes 196616 | tf_op jit(solution)/shard_map/ppermute | solution.py:14
  343.0 20.1 %copy-start.1 = (bf16[128,256]{1,0:T(8,128)(2,1)S(1)}, bf16[128,256]{1,0:T(8,128)(2,1)}, u32[]{:S(2)}) copy-start(bf16[128,256]{1,0:T(8,128)(2,1)} %param.14) | copy-start | bytes 196612
  343.0 20.1 %copy-start.2 = (bf16[128,256]{1,0:T(8,128)(2,1)S(1)}, bf16[128,256]{1,0:T(8,128)(2,1)}, u32[]{:S(2)}) copy-start(bf16[128,256]{1,0:T(8,128)(2,1)} %param.13) | copy-start | bytes 196612
Sparse Core Ops, SparseCore 0:
  11.0 79.5 all-gather.8
  92.8 74.2 all-gather.6
  262.4 80.5 all-gather.10
where the time goes:
time: 371 us
  waiting for transfers between devices  240 us (65%)
  blocking collectives  60.3 us (16%)
  other arithmetic  41.2 us (11%)
  between operations  14 us (4%)
  matrix products  8.16 us (2%)
    all_gather x1, waiting for transfers between devices, body(): backward_piece = lax.all_gather(back_spec[None], 'seq', axis=0, tiled=True)  78.4 us
    all_gather x1, waiting for transfers between devices, body(): filt_spec = lax.all_gather(own_spec[None], 'seq', axis=0, tiled=True)  77.7 us
    all_gather x1, waiting for transfers between devices, body(): piece = lax.all_gather(data_spec[None], 'seq', axis=0, tiled=True)  76.4 us
    psum x1, blocking collectives, body(): lax.psum((jnp.sum(resid * resid, axis=1, keepdims=True), jnp.sum(scaled *...  60.3 us
    convert_element_type x16, other arithmetic, backward_one_block(): taps.astype(jnp.float32)  16.2 us
    convert_element_type x16, other arithmetic, forward_one_block(): taps.astype(jnp.float32)  16.2 us
    dot_general x5, matrix products, matmul_high(): jnp.dot(left, right, precision=HIGHEST_MODE, preferred_element_type=jnp.f...  8.16 us
  transfers between devices with their start and end apart: 5, of which 5 were waited for; matrix products, arithmetic and copies ran while one was open for 1% of the time, Pallas kernels for 0%

commit v1 on v0

--- a/solution.py
+++ b/solution.py
@@ -76,7 +76,9 @@
     mixed = inner * value_rows
     data_spec = matmul_high(forward_half, mixed).astype(jnp.bfloat16)
     own_spec = matmul_high(forward_half, long_filter.astype(jnp.float32)).astype(jnp.bfloat16)
-    filt_spec = lax.all_gather(own_spec[None], "seq", axis=0, tiled=True)
+    filt_spec = jnp.concatenate(
+        lax.all_to_all(jnp.stack([own_spec[None]] * lax.axis_size("seq")), "seq", 0, 0), axis=0
+    )
     zero_total = jnp.zeros((2 * half, width), jnp.float32)
     piece = lax.all_gather(data_spec[None], "seq", axis=0, tiled=True)
 

time: 371 us -> 325 us (0.88)
  waiting for transfers between devices: 240 us -> 185 us
  starting transfers between devices: 2.94 us -> 10.9 us
    all_gather x1 -> x0, waiting for transfers between devices: 77.7 us -> none  [body(): filt_spec = lax.all_gather(own_spec[None], 'seq', axis=0, tiled=True)]
    all_to_all x0 -> x1, waiting for transfers between devices: none -> 52.5 us  [body(): lax.all_to_all(jnp.stack([own_spec[None]] * lax.axis_size('seq')), 'seq',...]
    all_gather x1, waiting for transfers between devices: 76.4 us -> 48.9 us  [body(): piece = lax.all_gather(data_spec[None], 'seq', axis=0, tiled=True)]
    all_to_all x0 -> x1, starting transfers between devices: none -> 7.97 us  [body(): lax.all_to_all(jnp.stack([own_spec[None]] * lax.axis_size('seq')), 'seq',...]
where the time goes in v1:
time: 325 us; the launch traced here: 324 us
  waiting for transfers between devices  185 us (57%)
  blocking collectives  62.1 us (19%)
  other arithmetic  39.1 us (12%)
  between operations  14.3 us (4%)
  starting transfers between devices  10.9 us (3%)
  matrix products  6.61 us (2%)
  local copies, waits for them, and re-layouts  4.11 us (1%)
    all_gather x1, waiting for transfers between devices, body(): backward_piece = lax.all_gather(back_spec[None], 'seq', axis=0, tiled=True)  76.5 us
    psum x1, blocking collectives, body(): lax.psum((jnp.sum(resid * resid, axis=1, keepdims=True), jnp.sum(scaled *...  62.1 us
    all_to_all x1, waiting for transfers between devices, body(): lax.all_to_all(jnp.stack([own_spec[None]] * lax.axis_size('seq')), 'seq',...  52.5 us
    all_gather x1, waiting for transfers between devices, body(): piece = lax.all_gather(data_spec[None], 'seq', axis=0, tiled=True)  48.9 us
    convert_element_type x16, other arithmetic, backward_one_block(): taps.astype(jnp.float32)  15.1 us
    convert_element_type x16, other arithmetic, forward_one_block(): taps.astype(jnp.float32)  15.1 us
    all_to_all x1, starting transfers between devices, body(): lax.all_to_all(jnp.stack([own_spec[None]] * lax.axis_size('seq')), 'seq',...  7.97 us
    ppermute x2, waiting for transfers between devices, from_behind(): lax.ppermute(value, axis, [(source, source + steps) for source in range(f...  7.06 us
  transfers between devices with their start and end apart: 5, of which 5 were waited for; matrix products, arithmetic and copies ran while one was open for 1% of the time, Pallas kernels for 0%

profile of v1, /device:TPU:4, one launch (start us, length us, event | category | flops | bytes accessed | tf_op | source)
XLA Modules:
  0.0 323.8 jit_solution(7542669787765009900)
XLA Ops:
  7.2 2.7 select_multiply_fusion
  10.2 1.5 stack.3
  11.7 8.0 %all-to-all-start = ((bf16[16,1,256,256]{3,2,1,0:T(8,128)(2,1)}), bf16[16,1,256,256]{3,2,1,0:T(8,128)(2,1)S(1)}, u32[]{:S(2)}, u32[]{:S(2)}) async-start(bf16[16,1,256,256]{3,2,1,0:T(8,128)(2,1)} %stack.3), calls=%async_computation | async-start | bytes 4194304 | tf_op jit(solution)/shard_map/all_to_all | solution.py:80
  19.8 1.0 convolution_convert_fusion.2
  20.9 52.5 %all-to-all-done = bf16[16,1,256,256]{3,2,1,0:T(8,128)(2,1)S(1)} async-done(((bf16[16,1,256,256]{3,2,1,0:T(8,128)(2,1)}), bf16[16,1,256,256]{3,2,1,0:T(8,128)(2,1)S(1)}, u32[]{:S(2)}, u32[]{:S(2)}) %all-to-all-start) | async-done | bytes 2097184 | tf_op jit(solution)/shard_map/all_to_all | solution.py:80
  73.4 48.9 %all-gather.5.cloned.1.call-done = bf16[4096,256]{1,0:T(8,128)(2,1)} async-done(((bf16[256,256]{1,0:T(8,128)(2,1)}), bf16[4096,256]{1,0:T(8,128)(2,1)}) %all-gather.5.cloned.1.call-update) | async-done | bytes 2097168 | tf_op jit(solution)/shard_map/all_gather | solution.py:83
  122.3 18.8 %while.28 = (s32[]{:T(128)}, f32[256,256]{1,0:T(8,128)S(1)}, s32[]{:T(128)}, bf16[16,256,256]{2,1,0:T(8,128)(2,1)}, bf16[16,256,256]{2,1,0:T(8,128)(2,1)S(1)}, /*index=5*/s32[]{:T(128)}, s32[]{:T(128)}, s32[]{:T(128)}) while((s32[]{:T(128)}, f32[256,256]{1,0:T(8,128)S(1)}, s32[]{:T(128)}, bf16[16,256,256]{2,1,0:T(8,128)(2,1)}, ...), condition=%wide.region_1.2_spmd.clone, body=%wide.region_0.1_spmd.clone.sunk | while | flops 655495 | bytes 2359701 | solution.py:92
  122.3 0.9 dynamic-slice_convert_fusion.6
  123.5 0.9 dynamic-slice_convert_fusion.6
  124.6 0.9 dynamic-slice_convert_fusion.6
  125.8 0.9 dynamic-slice_convert_fusion.6
  127.0 0.9 dynamic-slice_convert_fusion.6
  128.2 0.9 dynamic-slice_convert_fusion.6
  129.3 0.9 dynamic-slice_convert_fusion.6
  130.5 0.9 dynamic-slice_convert_fusion.6
  131.7 0.9 dynamic-slice_convert_fusion.6
  132.9 0.9 dynamic-slice_convert_fusion.6
  134.0 0.9 dynamic-slice_convert_fusion.6
  135.2 0.9 dynamic-slice_convert_fusion.6
  136.4 0.9 dynamic-slice_convert_fusion.6
  137.6 0.9 dynamic-slice_convert_fusion.6
  138.7 0.9 dynamic-slice_convert_fusion.6
  139.9 0.9 dynamic-slice_convert_fusion.6
  141.1 2.2 fusion.23
  143.3 1.6 collective-permute-start
  145.2 1.5 collective-permute-done
  146.9 62.1 %all-reduce = (f32[128,1]{0,1:T(1,128)S(1)}, f32[128,1]{0,1:T(1,128)S(1)}) all-reduce(f32[128,1]{0,1:T(1,128)S(1)} %bitcast.65, f32[128,1]{0,1:T(1,128)S(1)} %bitcast.64), channel_id=1, replica_groups=mesh['seq'=16,'chan'=32] {'chan'}, use_global_device_ids=true, to_apply=%region_3.4 | all-reduce | flops 256 | bytes 2048 | tf_op jit(solution)/shard_map/psum | solution.py:98
  209.1 1.3 collective-permute-start.1
  210.4 5.6 %collective-permute-done.1 = bf16[128,256]{0,1:T(8,128)(2,1)S(1)} collective-permute-done((bf16[128,256]{0,1:T(8,128)(2,1)S(1)}, bf16[128,256]{0,1:T(8,128)(2,1)S(1)}, u32[]{:S(2)}, u32[]{:S(2)}) %collective-permute-start.1) | collective-permute-done | bytes 65568 | tf_op jit(solution)/shard_map/ppermute | solution.py:14
  216.0 2.2 convolution_convert_fusion
  220.5 76.5 %all-gather.7.cloned.1.call-done = bf16[4096,256]{1,0:T(8,128)(2,1)} async-done(((bf16[256,256]{1,0:T(8,128)(2,1)}), bf16[4096,256]{1,0:T(8,128)(2,1)}) %all-gather.7.cloned.1.call-update) | async-done | bytes 2097168 | tf_op jit(solution)/shard_map/all_gather | solution.py:115
  297.0 19.1 %while.29 = (s32[]{:T(128)}, f32[256,256]{1,0:T(8,128)S(1)}, s32[]{:T(128)}, bf16[16,256,256]{2,1,0:T(8,128)(2,1)}, bf16[16,256,256]{2,1,0:T(8,128)(2,1)S(1)}, /*index=5*/s32[]{:T(128)}, s32[]{:T(128)}, s32[]{:T(128)}) while((s32[]{:T(128)}, f32[256,256]{1,0:T(8,128)S(1)}, s32[]{:T(128)}, bf16[16,256,256]{2,1,0:T(8,128)(2,1)}, ...), condition=%wide.region_7.8_spmd.clone, body=%wide.region_6.7_spmd.clone.sunk | while | flops 753799 | bytes 2359701 | solution.py:124
  298.1 0.9 dynamic-slice_convert_fusion.7
  299.3 0.9 dynamic-slice_convert_fusion.7
  300.5 0.9 dynamic-slice_convert_fusion.7
  301.7 0.9 dynamic-slice_convert_fusion.7
  302.9 0.9 dynamic-slice_convert_fusion.7
  304.1 0.9 dynamic-slice_convert_fusion.7
  305.3 0.9 dynamic-slice_convert_fusion.7
  306.5 0.9 dynamic-slice_convert_fusion.7
  307.7 0.9 dynamic-slice_convert_fusion.7
  308.9 0.9 dynamic-slice_convert_fusion.7
  310.1 0.9 dynamic-slice_convert_fusion.7
  311.3 0.9 dynamic-slice_convert_fusion.7
  312.5 0.9 dynamic-slice_convert_fusion.7
  313.7 0.9 dynamic-slice_convert_fusion.7
  314.8 0.9 dynamic-slice_convert_fusion.7
  316.0 0.9 fusion.13
  (135 shorter events, 10.1 us)
Async XLA Ops:
  7.2 2.8 copy-start
  11.7 8.0 %copy-start.1 = (bf16[128,256]{1,0:T(8,128)(2,1)S(1)}, bf16[128,256]{1,0:T(8,128)(2,1)}, u32[]{:S(2)}) copy-start(bf16[128,256]{1,0:T(8,128)(2,1)} %param.14) | copy-start | bytes 196612
  11.7 8.0 %copy-start.2 = (bf16[128,256]{1,0:T(8,128)(2,1)S(1)}, bf16[128,256]{1,0:T(8,128)(2,1)}, u32[]{:S(2)}) copy-start(bf16[128,256]{1,0:T(8,128)(2,1)} %param.13) | copy-start | bytes 196612
  11.7 61.7 %all-to-all-start = ((bf16[16,1,256,256]{3,2,1,0:T(8,128)(2,1)}), bf16[16,1,256,256]{3,2,1,0:T(8,128)(2,1)S(1)}, u32[]{:S(2)}, u32[]{:S(2)}) async-start(bf16[16,1,256,256]{3,2,1,0:T(8,128)(2,1)} %stack.3), calls=%async_computation | async-start | bytes 4194304 | tf_op jit(solution)/shard_map/all_to_all | solution.py:80
  19.7 102.6 %all-gather.5.cloned.1.call-start = ((), (), s32[]{:S(2)}) async-start(), calls=%async_computation.1 | async-start | bytes 2228224 | tf_op jit(solution)/shard_map/all_gather | solution.py:83
  20.8 276.2 %all-gather.7.cloned.1.call-start = ((), (), s32[]{:S(2)}) async-start(), calls=%async_computation.2 | async-start | bytes 2228224 | tf_op jit(solution)/shard_map/all_gather | solution.py:115
  141.1 3.8 %copy-start.3 = (bf16[128,256]{1,0:T(8,128)(2,1)S(1)}, bf16[128,256]{1,0:T(8,128)(2,1)}, u32[]{:S(2)}) copy-start(bf16[128,256]{1,0:T(8,128)(2,1)} %param.12) | copy-start | bytes 196612
  141.1 3.9 %copy-start.4 = (bf16[128,256]{1,0:T(8,128)(2,1)S(1)}, bf16[128,256]{1,0:T(8,128)(2,1)}, u32[]{:S(2)}) copy-start(bf16[128,256]{1,0:T(8,128)(2,1)} %param.17) | copy-start | bytes 196612
  141.1 4.0 %copy-start.5 = (bf16[128,256]{1,0:T(8,128)(2,1)S(1)}, bf16[128,256]{1,0:T(8,128)(2,1)}, u32[]{:S(2)}) copy-start(bf16[128,256]{1,0:T(8,128)(2,1)} %param.11) | copy-start | bytes 196612
  141.1 5.6 %copy-start.6 = (f32[256]{0:T(256)S(1)}, f32[256]{0:T(256)}, u32[]{:S(2)}) copy-start(f32[256]{0:T(256)} %param.16) | copy-start | bytes 3076
  143.3 3.4 %collective-permute-start = (bf16[128,256]{0,1:T(8,128)(2,1)S(1)}, bf16[128,256]{0,1:T(8,128)(2,1)S(1)}, u32[]{:S(2)}, u32[]{:S(2)}) collective-permute-start(bf16[128,256]{0,1:T(8,128)(2,1)S(1)} %slice.167), channel_id=1, source_target_pairs={{0,32},{32,64},{64,96},{96,128},{128,160},{160,192},{192,224},{224... | collective-permute-start | bytes 196616 | tf_op jit(solution)/shard_map/ppermute | solution.py:14
  209.1 6.9 %collective-permute-start.1 = (bf16[128,256]{0,1:T(8,128)(2,1)S(1)}, bf16[128,256]{0,1:T(8,128)(2,1)S(1)}, u32[]{:S(2)}, u32[]{:S(2)}) collective-permute-start(bf16[128,256]{0,1:T(8,128)(2,1)S(1)} %get-tuple-element.265), channel_id=1, source_target_pairs={{32,0},{64,32},{96,64},{128,96},{160,128},{192,160},{224,192},{256... | collective-permute-start | bytes 196616 | tf_op jit(solution)/shard_map/ppermute | solution.py:14
Sparse Core Ops, SparseCore 0:
  22.6 99.6 all-gather.4
  218.4 78.5 all-gather.6
